TPU v7x, 512 devices: a whole 4x4x16 slice. The times are simulated.
512 devices in a mesh: fibre: 32 (over z, core), group: 16 (over y, x).
Axes of the slice: x: 4, y: 4, z: 16, core: 2. Of those that a mesh axis runs over, the one named last changes fastest.
Arguments:
- species_field: float32 [512, 524288], P('fibre', 'group'), may hold values from -45 to 45, as said below
- start_block: float32 [512, 64], replicated, may hold values from -4 to 4
Outputs:
- mode_basis: float32 [512, 64], replicated
- core_tensor: float32 [64, 524288], P(None, ('group', 'fibre'))
Inputs may be any that keep to these rules, and one draw needn't show every extreme that they name: `species_field`: float32 field values.
All inputs are finite; a program needn't handle non-finite values.
Results may differ from a plain program's by a relative error of at most 0.0003.
Values sent between devices are 32-bit elements; how exact they have to be, the bound alone decides.
No kernel may reach another device: no remote copies, remote signals or barrier semaphores. Data moves between devices by JAX's collectives and lax.ppermute only.
A program may use at most 64 MiB of HBM per device.

v0:
```python
import jax
import jax.numpy as jnp
from jax import lax
from jax.sharding import PartitionSpec as P

ITERS = 3
highest_precision = lax.Precision.HIGHEST


def orthonormal(matrix):
    inner_gram = jnp.dot(matrix.T, matrix, precision=highest_precision)
    lower_factor = jnp.linalg.cholesky(inner_gram)
    return lax.linalg.triangular_solve(
        lower_factor, matrix, left_side=False, lower=True, transpose_a=True
    )


def on_device(species_field, start_block):
    fibres = lax.all_to_all(species_field, "fibre", split_axis=1, concat_axis=0, tiled=True)
    total_columns = fibres.shape[1] * lax.axis_size("fibre") * lax.axis_size("group")
    mode_basis = orthonormal(start_block)
    local_gram = jnp.dot(fibres, fibres.T, precision=highest_precision) / total_columns
    gram_matrix = lax.psum(local_gram, ("fibre", "group"))
    for iteration in range(ITERS):
        mode_basis = orthonormal(jnp.dot(gram_matrix, mode_basis, precision=highest_precision))
    core_tensor = jnp.dot(mode_basis.T, fibres, precision=highest_precision)
    return (mode_basis, core_tensor)


def solution(mesh):
    placed = (P("fibre", "group"), P())
    return jax.shard_map(
        on_device,
        mesh=mesh,
        in_specs=placed,
        out_specs=(P(), P(None, ("group", "fibre"))),
        check_vma=False,
    )
```

profile of v0, /device:TPU:1, one launch (start us, length us, event | category | flops | bytes accessed | tf_op | source)
XLA Modules:
  0.0 643.5 jit_solution(7276870236529994059)
XLA Ops:
  7.2 3.2 copy.24
  10.4 16.7 %all-to-all-start = ((f32[16,32,1024]{2,0,1:T(8,128)}), f32[16,32,1024]{2,0,1:T(8,128)S(1)}, u32[]{:S(2)}, u32[]{:S(2)}) async-start(f32[16,32,1024]{2,0,1:T(8,128)} %bitcast.75), calls=%async_computation | async-start | bytes 4194304 | tf_op jit(solution)/shard_map/all_to_all | solution.py:19
  27.6 5.8 cholesky.74
  33.5 92.3 %all-to-all-done = f32[16,32,1024]{2,0,1:T(8,128)S(1)} async-done(((f32[16,32,1024]{2,0,1:T(8,128)}), f32[16,32,1024]{2,0,1:T(8,128)S(1)}, u32[]{:S(2)}, u32[]{:S(2)}) %all-to-all-start) | async-done | bytes 2097184 | tf_op jit(solution)/shard_map/all_to_all | solution.py:19
  125.8 4.6 convolution_multiply_fusion
  130.4 0.6 compare_reduce_fusion.3
  131.0 0.7 fusion
  131.6 4.9 custom-call.8
  136.5 0.3 convolution_bitcast_fusion.3
  136.9 454.4 %all-reduce.2.cloned.1.call-done = f32[512,512]{1,0:T(8,128)} async-done(((f32[512,512]{1,0:T(8,128)}), f32[512,512]{1,0:T(8,128)}) %all-reduce.2.cloned.1.call-update) | async-done | bytes 1048592 | tf_op jit(solution)/shard_map/psum | solution.py:23
  591.3 2.4 fusion.19
  593.7 0.3 fusion.20
  594.1 5.8 cholesky.85
  600.0 0.6 compare_reduce_fusion.2
  600.6 0.7 fusion.1
  601.3 4.9 custom-call.9
  606.2 0.3 convolution_bitcast_fusion.2
  606.5 1.1 fusion.21
  607.6 0.3 fusion.22
  608.0 5.8 cholesky.96
  613.9 0.6 compare_reduce_fusion.1
  614.5 0.7 fusion.2
  615.2 4.9 custom-call.10
  620.1 0.3 convolution_bitcast_fusion.1
  620.4 1.3 fusion.23
  621.8 0.3 fusion.24
  622.1 5.8 cholesky.107
  628.0 0.6 compare_reduce_fusion
  628.6 0.7 fusion.3
  629.3 4.9 custom-call.11
  634.2 0.3 convolution_bitcast_fusion
  634.6 2.1 fusion.25
  (21 shorter events, 0.8 us)
Async XLA Ops:
  7.2 20.0 %copy-start = (f32[512,64]{0,1:T(8,128)S(1)}, f32[512,64]{0,1:T(8,128)}, u32[]{:S(2)}) copy-start(f32[512,64]{0,1:T(8,128)} %param.6) | copy-start | bytes 393220
  10.4 115.4 %all-to-all-start = ((f32[16,32,1024]{2,0,1:T(8,128)}), f32[16,32,1024]{2,0,1:T(8,128)S(1)}, u32[]{:S(2)}, u32[]{:S(2)}) async-start(f32[16,32,1024]{2,0,1:T(8,128)} %bitcast.75), calls=%async_computation | async-start | bytes 4194304 | tf_op jit(solution)/shard_map/all_to_all | solution.py:19
  27.2 564.1 %all-reduce.2.cloned.1.call-start = ((), (), s32[]{:S(2)}) async-start(), calls=%async_computation.1 | async-start | bytes 2097152 | tf_op jit(solution)/shard_map/psum | solution.py:23
  591.3 15.2 %copy-start.1 = (f32[512,512]{1,0:T(8,128)S(1)}, f32[512,512]{1,0:T(8,128)}, u32[]{:S(2)}) copy-start(f32[512,512]{1,0:T(8,128)} %all-reduce.2.cloned.1.call-done) | copy-start | bytes 3145732
  634.5 2.1 copy-start.2
Sparse Core Ops, SparseCore 0:
  130.5 460.7 all-reduce.1
where the time goes:
time: 644 us; the launch traced here: 643 us
  waiting for transfers between devices  547 us (85%)
  other arithmetic  48.3 us (8%)
  starting transfers between devices  16.8 us (3%)
  between operations  14.2 us (2%)
  matrix products  13.9 us (2%)
    psum x1, waiting for transfers between devices, on_device(): gram_matrix = lax.psum(local_gram, ('fibre', 'group'))  454 us
    all_to_all x1, waiting for transfers between devices, on_device(): lax.all_to_all(species_field, 'fibre', split_axis=1, concat_axis=0, tiled...  92.3 us
    another operation x12, other arithmetic, orthonormal(): lower_factor = jnp.linalg.cholesky(inner_gram)  26.1 us
    another operation x8, other arithmetic, orthonormal(): lax.linalg.triangular_solve(lower_factor, matrix, left_side=False, lower=...  22.2 us
    all_to_all x1, starting transfers between devices, on_device(): lax.all_to_all(species_field, 'fibre', split_axis=1, concat_axis=0, tiled...  16.7 us
  transfers between devices with their start and end apart: 2, of which 2 were waited for; matrix products, arithmetic and copies ran while one was open for 2% of the time, Pallas kernels for 0%

commit v1 on v0

--- a/solution.py
+++ b/solution.py
@@ -20,7 +20,7 @@
     total_columns = fibres.shape[1] * lax.axis_size("fibre") * lax.axis_size("group")
     mode_basis = orthonormal(start_block)
     local_gram = jnp.dot(fibres, fibres.T, precision=highest_precision) / total_columns
-    gram_matrix = lax.psum(local_gram, ("fibre", "group"))
+    gram_matrix = lax.psum(lax.psum(local_gram, "fibre"), "group")
     for iteration in range(ITERS):
         mode_basis = orthonormal(jnp.dot(gram_matrix, mode_basis, precision=highest_precision))
     core_tensor = jnp.dot(mode_basis.T, fibres, precision=highest_precision)

time: 644 us -> 505 us (0.78)
  waiting for transfers between devices: 547 us -> 309 us
  blocking collectives: 0 us -> 117 us
  starting transfers between devices: 16.8 us -> 0.26 us
    psum x1 -> x2, waiting for transfers between devices: 454 us -> 309 us  [on_device(): gram_matrix = lax.psum(lax.psum(local_gram, 'fibre'), 'group')]
    all_to_all x0 -> x1, blocking collectives: none -> 117 us  [on_device(): lax.all_to_all(species_field, 'fibre', split_axis=1, concat_axis=0, tiled...]
    all_to_all x1 -> x0, waiting for transfers between devices: 92.3 us -> none  [on_device(): lax.all_to_all(species_field, 'fibre', split_axis=1, concat_axis=0, tiled...]
    all_to_all x1 -> x0, starting transfers between devices: 16.7 us -> none  [on_device(): lax.all_to_all(species_field, 'fibre', split_axis=1, concat_axis=0, tiled...]
  transfers between devices with their start and end apart: 2 -> 2, of which waited for: 2 -> 2; matrix products, arithmetic and copies ran while one was open for 2% -> 3% of each run, Pallas kernels for 0% -> 0%
where the time goes in v1:
time: 505 us
  waiting for transfers between devices  309 us (61%)
  blocking collectives  117 us (23%)
  other arithmetic  48.3 us (10%)
  between operations  14.2 us (3%)
  matrix products  13.8 us (3%)
    psum x2, waiting for transfers between devices, on_device(): gram_matrix = lax.psum(lax.psum(local_gram, 'fibre'), 'group')  309 us
    all_to_all x1, blocking collectives, on_device(): lax.all_to_all(species_field, 'fibre', split_axis=1, concat_axis=0, tiled...  117 us
    another operation x12, other arithmetic, orthonormal(): lower_factor = jnp.linalg.cholesky(inner_gram)  26.1 us
    another operation x8, other arithmetic, orthonormal(): lax.linalg.triangular_solve(lower_factor, matrix, left_side=False, lower=...  22.2 us
  transfers between devices with their start and end apart: 2, of which 2 were waited for; matrix products, arithmetic and copies ran while one was open for 3% of the time, Pallas kernels for 0%

profile of v1, /device:TPU:1, one launch (start us, length us, event | category | flops | bytes accessed | tf_op | source)
XLA Modules:
  0.0 504.5 jit_solution(4016844151795974575)
XLA Ops:
  7.2 1.8 copy.24
  9.0 117.2 %all_to_all.19 = f32[16,32,1024]{2,0,1:T(8,128)S(1)} all-to-all(f32[16,32,1024]{2,0,1:T(8,128)S(1)} %bitcast.75), channel_id=1, replica_groups=mesh['fibre'=32,'group'=16] {'fibre'}, dimensions={1} | all-to-all | bytes 4194304 | tf_op jit(solution)/shard_map/all_to_all | solution.py:19
  126.2 4.6 convolution_multiply_fusion
  131.0 201.8 %all-reduce.3.cloned.1.call-done = f32[512,512]{1,0:T(8,128)} async-done(((f32[512,512]{1,0:T(8,128)}), f32[512,512]{1,0:T(8,128)}) %all-reduce.3.cloned.1.call-update) | async-done | bytes 1048592 | tf_op jit(solution)/shard_map/psum | solution.py:23
  333.2 5.8 %cholesky.74 = f32[64,64]{1,0:T(8,128)S(1)} custom-call(f32[64,64]{1,0:T(8,128)S(1)} %fusion.11), custom_call_target="Cholesky" | custom-call | tf_op jit(solution)/shard_map/jit(cholesky)/cholesky | solution.py:12
  339.1 0.6 compare_reduce_fusion.3
  339.7 0.7 fusion
  340.4 4.9 custom-call.8
  345.3 0.3 convolution_bitcast_fusion.3
  345.6 106.9 %all-reduce.5.cloned.1.call-done = f32[512,512]{1,0:T(8,128)} async-done(((f32[512,512]{1,0:T(8,128)}), f32[512,512]{1,0:T(8,128)}) %all-reduce.5.cloned.1.call-update) | async-done | bytes 1048592 | tf_op jit(solution)/shard_map/psum | solution.py:23
  452.5 2.4 fusion.19
  454.9 0.3 fusion.20
  455.3 5.8 %cholesky.85 = f32[64,64]{1,0:T(8,128)S(1)} custom-call(f32[64,64]{1,0:T(8,128)S(1)} %fusion.9), custom_call_target="Cholesky" | custom-call | tf_op jit(solution)/shard_map/jit(cholesky)/cholesky | solution.py:12
  461.2 0.6 compare_reduce_fusion.2
  461.8 0.7 fusion.1
  462.5 4.9 custom-call.9
  467.4 0.3 convolution_bitcast_fusion.2
  467.7 1.1 fusion.21
  468.9 0.3 fusion.22
  469.2 5.8 %cholesky.96 = f32[64,64]{1,0:T(8,128)S(1)} custom-call(f32[64,64]{1,0:T(8,128)S(1)} %fusion.7), custom_call_target="Cholesky" | custom-call | tf_op jit(solution)/shard_map/jit(cholesky)/cholesky | solution.py:12
  475.1 0.6 compare_reduce_fusion.1
  475.8 0.7 fusion.2
  476.4 4.9 custom-call.10
  481.3 0.3 convolution_bitcast_fusion.1
  481.7 1.1 fusion.23
  482.8 0.3 fusion.24
  483.2 5.8 %cholesky.107 = f32[64,64]{1,0:T(8,128)S(1)} custom-call(f32[64,64]{1,0:T(8,128)S(1)} %fusion.5), custom_call_target="Cholesky" | custom-call | tf_op jit(solution)/shard_map/jit(cholesky)/cholesky | solution.py:12
  489.0 0.6 compare_reduce_fusion
  489.7 0.7 fusion.3
  490.3 4.9 custom-call.11
  495.2 0.3 convolution_bitcast_fusion
  495.6 2.1 fusion.25
  (23 shorter events, 1.0 us)
Async XLA Ops:
  7.2 325.7 %copy-start = (f32[512,64]{0,1:T(8,128)S(1)}, f32[512,64]{0,1:T(8,128)}, u32[]{:S(2)}) copy-start(f32[512,64]{0,1:T(8,128)} %param.6) | copy-start | bytes 393220
  7.2 325.6 %all-reduce.3.cloned.1.call-start = ((), (), s32[]{:S(2)}) async-start(), calls=%async_computation.1 | async-start | bytes 2097152 | tf_op jit(solution)/shard_map/psum | solution.py:23
  130.8 321.7 %all-reduce.5.cloned.1.call-start = ((), (), s32[]{:S(2)}) async-start(), calls=%async_computation.2 | async-start | bytes 2097152 | tf_op jit(solution)/shard_map/psum | solution.py:23
  452.5 15.2 %copy-start.1 = (f32[512,512]{1,0:T(8,128)S(1)}, f32[512,512]{1,0:T(8,128)}, u32[]{:S(2)}) copy-start(f32[512,512]{1,0:T(8,128)} %all-reduce.5.cloned.1.call-done) | copy-start | bytes 3145732
  495.6 2.1 copy-start.2
Sparse Core Ops, SparseCore 0:
  130.9 201.8 all-reduce.2
  336.4 116.0 all-reduce.4
